TPU v7x, 32 devices: a whole 2x2x4 slice. The times are simulated.
32 devices in a mesh: ep: 16 (over z, x, core), dp: 2 (over y).
Axes of the slice: x: 2, y: 2, z: 4, core: 2. Of those that a mesh axis runs over, the one named last changes fastest.
Arguments:
- tokens: bfloat16 [1024, 4096], P('ep', 'dp'), may hold values from -6 to 6
- expert_ids: int32 [1024, 8], P('ep'), may hold values from 0 to 15, all different within a row
- gate_logits: float32 [1024, 8], P('ep'), may hold values from -6 to 6
- placement: int32 [8], replicated, may hold values from 0 to 15, as said below
- split_rows: int32 [8], replicated, may hold values from 0 to 32
- gate_up_weight: bfloat16 [16, 4096, 2, 1024], P('ep', None, None, 'dp'), may hold values from -0.09375 to 0.09375
- down_weight: bfloat16 [16, 1024, 4096], P('ep', None, 'dp'), may hold values from -0.1875 to 0.1875
- spare_gate_up: bfloat16 [16, 4096, 2, 512], P('ep', None, None, 'dp'), may hold values from -0.09375 to 0.09375
- spare_down: bfloat16 [16, 512, 4096], P('ep', None, 'dp'), may hold values from -0.1875 to 0.1875
Outputs:
- mixed: bfloat16 [1024, 4096], P('ep', 'dp')
Inputs may be any that keep to these rules, and one draw needn't show every extreme that they name: `expert_ids`: each token names 8 different experts. `placement`: 8 different experts.
All inputs are finite; a program needn't handle non-finite values.
Results may differ from a plain program's by a relative error of at most 0.0058.
Values may be sent and summed in bfloat16 or wider, within the bound.
No kernel may reach another device: no remote copies, remote signals or barrier semaphores. Data moves between devices by JAX's collectives and lax.ppermute only.
A program may use at most 64 MiB of HBM per device.

v0:
```python
import jax
import jax.numpy as jnp
from jax import lax
from jax.sharding import PartitionSpec as P


def gate_up(row_block, weight):
    gate_both = jnp.einsum("rd,djf->rjf", row_block, weight, preferred_element_type=jnp.float32)
    return (jax.nn.silu(gate_both[:, 0, :]) * gate_both[:, 1, :]).astype(jnp.bfloat16)


def slot_tables(ids, target, low, limit, capacity, top_count, gate_weight):
    groups, per_group = ids.shape
    group_tokens = per_group // top_count
    hit = ids == target
    ordinal = jnp.arange(per_group, dtype=jnp.int32)
    earlier = (ordinal[None, :] < ordinal[:, None]).astype(jnp.bfloat16)
    rank = jnp.einsum(
        "pq,gq->gp", earlier, hit.astype(jnp.bfloat16), preferred_element_type=jnp.float32
    ).astype(jnp.int32)
    position = rank - low
    kept = hit & (position >= 0) & (position < limit)
    slots = jnp.arange(capacity, dtype=jnp.int32)
    sel = kept[:, :, None] & (position[:, :, None] == slots[None, None, :])
    holds = jnp.any(sel.reshape(groups, group_tokens, top_count, capacity), axis=2)
    pick = jnp.transpose(holds, (0, 2, 1)).astype(jnp.bfloat16)
    scale = jnp.sum(
        jnp.where(kept.reshape(groups * group_tokens, top_count), gate_weight, 0.0), axis=1
    )
    return (pick, holds.astype(jnp.bfloat16), scale)


def side_columns(expert_ids, gate_logits):
    high = gate_logits.astype(jnp.bfloat16)
    rest = gate_logits - high.astype(jnp.float32)
    middle = rest.astype(jnp.bfloat16)
    low = (rest - middle.astype(jnp.float32)).astype(jnp.bfloat16)
    columns = jnp.concatenate([expert_ids.astype(jnp.bfloat16), high, middle, low], axis=1)
    width = -columns.shape[1] % 128
    return jnp.pad(columns, ((0, 0), (0, width)))


def gather_dp(block, axis):
    if lax.axis_size("dp") != 2:
        return lax.all_gather(block, "dp", axis=axis, tiled=True)
    partner = lax.ppermute(block, "dp", perm=[(0, 1), (1, 0)])
    first = lax.axis_index("dp") == 0
    low = jnp.where(first, block, partner)
    high = jnp.where(first, partner, block)
    return jnp.concatenate([low, high], axis=axis)


def down_dp(hidden, weight):
    if lax.axis_size("dp") != 2:
        gathered = lax.all_gather(hidden, "dp", axis=1, tiled=True)
        return jnp.dot(gathered, weight, preferred_element_type=jnp.float32)
    partner = lax.ppermute(hidden, "dp", perm=[(0, 1), (1, 0)])
    blocks = weight.reshape(2, hidden.shape[1], weight.shape[1])
    first = lax.axis_index("dp") == 0
    own = jnp.where(first, blocks[0], blocks[1])
    other = jnp.where(first, blocks[1], blocks[0])
    return jnp.dot(hidden, own, preferred_element_type=jnp.float32) + jnp.dot(
        partner, other, preferred_element_type=jnp.float32
    )


def per_device(
    tokens,
    expert_ids,
    gate_logits,
    placement,
    split_rows,
    gate_up_weight,
    down_weight,
    spare_gate_up,
    spare_down,
):
    ep_count = lax.axis_size("ep")
    me = lax.axis_index("ep")
    group_tokens = tokens.shape[0]
    top_count = expert_ids.shape[1]
    spares = placement.shape[0]
    halves = spare_gate_up.shape[0] * ep_count // spares
    capacity = group_tokens * top_count // ep_count
    per_group = group_tokens * top_count
    d_model = tokens.shape[1] * lax.axis_size("dp")
    whole_rows = gather_dp(tokens, 1)
    packed = jnp.concatenate([whole_rows, side_columns(expert_ids, gate_logits)], axis=1)
    every_row = lax.all_gather(packed, "ep", axis=0, tiled=True)
    all_tokens = every_row.shape[0]
    ids = every_row[:, d_model : d_model + top_count].astype(jnp.int32)
    parts = every_row[:, d_model + top_count : d_model + 4 * top_count].astype(jnp.float32)
    every_logit = (
        parts[:, :top_count] + parts[:, top_count : 2 * top_count] + parts[:, 2 * top_count :]
    )
    ids = ids.reshape(ep_count, per_group)
    gate_score = jax.nn.sigmoid(every_logit)
    gate_weight = 2.5 * gate_score / jnp.sum(gate_score, axis=1, keepdims=True)
    is_match = placement == me
    home_limit = jnp.where(
        jnp.any(is_match),
        jnp.minimum(jnp.sum(jnp.where(is_match, split_rows, 0)), capacity),
        capacity,
    )
    home_pick, home_take, home_scale = slot_tables(
        ids, me, 0, home_limit, capacity, top_count, gate_weight
    )
    spare_index = me // halves
    spare_pick, spare_take, spare_scale = slot_tables(
        ids,
        placement[spare_index],
        split_rows[spare_index],
        capacity,
        capacity,
        top_count,
        gate_weight,
    )
    grouped = every_row.reshape(ep_count, group_tokens, -1)
    slot_rows = ep_count * capacity
    rows = jnp.einsum(
        "gpi,gic->gpc",
        jnp.concatenate([home_pick, spare_pick], axis=1),
        grouped,
        preferred_element_type=jnp.float32,
    ).astype(jnp.bfloat16)
    home_rows = rows[:, :capacity].reshape(slot_rows, -1)
    spare_rows = rows[:, capacity:].reshape(slot_rows, -1)
    home_hidden = gate_up(home_rows[:, :d_model], gate_up_weight[0])
    home_hidden, spare_rows = lax.optimization_barrier((home_hidden, spare_rows))
    home_out = down_dp(home_hidden, down_weight[0])
    home_out = home_out.astype(jnp.bfloat16).reshape(ep_count, capacity, -1)
    spare_out = down_dp(gate_up(spare_rows[:, :d_model], spare_gate_up[0]), spare_down[0])
    spare_high = spare_out.astype(jnp.bfloat16)
    spare_low = (spare_out - spare_high.astype(jnp.float32)).astype(jnp.bfloat16)
    spare_high = spare_high.reshape(ep_count, capacity, -1)
    spare_low = spare_low.reshape(ep_count, capacity, -1)
    home_term = jnp.einsum(
        "gip,gpc->gic", home_take, home_out, preferred_element_type=jnp.float32
    ).reshape(all_tokens, -1)
    spare_term = jnp.einsum(
        "gip,gpc->gic",
        jnp.concatenate([spare_take, spare_take], axis=2),
        jnp.concatenate([spare_high, spare_low], axis=1),
        preferred_element_type=jnp.float32,
    ).reshape(all_tokens, -1)
    partial = home_scale[:, None] * home_term + spare_scale[:, None] * spare_term
    mixed = lax.psum_scatter(partial.astype(jnp.bfloat16), "ep", scatter_dimension=0, tiled=True)
    return mixed.astype(jnp.bfloat16)


def solution(mesh):
    return jax.shard_map(
        per_device,
        mesh=mesh,
        in_specs=(
            P("ep", "dp"),
            P("ep", None),
            P("ep", None),
            P(),
            P(),
            P("ep", None, None, "dp"),
            P("ep", None, "dp"),
            P("ep", None, None, "dp"),
            P("ep", None, "dp"),
        ),
        out_specs=P("ep", "dp"),
        check_vma=False,
    )
```

profile of v0, /device:TPU:0, one launch (start us, length us, event | category | flops | bytes accessed | tf_op | source)
XLA Modules:
  0.0 224.1 jit_solution(15065613179835285331)
XLA Ops:
  6.5 0.0 all-gather.2.cloned.1.call-start
  6.5 3.0 %collective-permute-start = (bf16[64,2048]{1,0:T(8,128)(2,1)}, bf16[64,2048]{1,0:T(8,128)(2,1)S(1)}, u32[]{:S(2)}, u32[]{:S(2)}) collective-permute-start(bf16[64,2048]{1,0:T(8,128)(2,1)} %param.9), channel_id=1, source_target_pairs={{0,1},{1,0},{2,3},{3,2},{4,5},{5,4},{6,7},{7,6},{8,9},{9,8},{10,11... | collective-permute-start | bytes 786440 | tf_op jit(solution)/shard_map/ppermute | solution.py:46
  9.5 0.7 convert_element_type.75
  10.2 0.8 fusion.67
  11.0 0.1 copy.56
  11.1 4.9 %collective-permute-done = bf16[64,2048]{1,0:T(8,128)(2,1)S(1)} collective-permute-done((bf16[64,2048]{1,0:T(8,128)(2,1)}, bf16[64,2048]{1,0:T(8,128)(2,1)S(1)}, u32[]{:S(2)}, u32[]{:S(2)}) %collective-permute-start) | collective-permute-done | bytes 262176 | tf_op jit(solution)/shard_map/ppermute | solution.py:46
  16.0 1.0 broadcast_select_fusion.1
  17.0 0.9 fusion.42
  17.9 0.0 all-gather.2.cloned.1.call-update
  17.9 0.0 reduce-scatter.2.cloned.1.call-start
  18.0 1.2 dynamic_slice.6
  19.2 1.3 dynamic_slice.7
  20.5 1.4 fusion.59
  22.6 1.4 compare_reduce_fusion
  24.6 71.5 %all-gather.2.cloned.1.call-done = bf16[1024,4224]{1,0:T(8,128)(2,1)} async-done(((bf16[64,4224]{1,0:T(8,128)(2,1)}), bf16[1024,4224]{1,0:T(8,128)(2,1)}) %all-gather.2.cloned.1.call-update) | async-done | bytes 8650768 | tf_op jit(solution)/shard_map/all_gather | solution.py:89
  96.1 1.8 convert_compare_fusion.1
  97.9 0.3 eq.64
  98.3 0.3 eq.73
  98.6 0.3 compare_and_fusion.1
  98.9 0.2 copy.44
  99.1 0.2 copy.45
  99.2 0.9 compare_and_fusion
  100.1 0.2 copy.48
  100.3 0.2 copy.49
  100.4 0.1 copy.46
  100.6 0.1 copy.47
  100.7 0.1 copy.50
  100.8 0.1 copy.51
  101.0 0.5 fusion.18
  101.5 0.5 fusion.20
  102.0 5.8 %convolution_convert_fusion = bf16[16,64,4224]{2,1,0:T(8,128)(2,1)S(1)} fusion(bf16[16,64,4224]{2,1,0:T(8,128)(2,1)} %bitcast.84, pred[16,32,64]{2,1,0:T(8,128)(4,1)S(1)} %bitcast.93, pred[16,32,64]{2,1,0:T(8,128)(4,1)S(1)} %bitcast.92), kind=kOutput, calls=%fused_computation | convolution fusion | flops 558039040 | bytes 17367040 | tf_op jit(solution)/shard_map/gpi,gic->gpc/dot_general | solution.py:120
  107.8 0.8 fusion.66
  108.6 0.0 copy-start.4
  108.7 7.3 %fusion.2 = f32[512,2,512]{2,0,1:T(8,128)S(1)} fusion(bf16[4096,2,512]{2,1,0:T(2,128)(2,1)} %bitcast.96, bf16[512,4224]{1,0:T(8,128)(2,1)S(1)} %bitcast.89), kind=kOutput, calls=%fused_computation.5 | convolution fusion | flops 4294967296 | bytes 14680064 | tf_op jit(solution)/shard_map/rd,djf->rjf/dot_general | solution.py:8
  115.9 1.1 fusion.30
  117.0 0.0 copy-done.4
  117.0 0.0 copy-start.1
  117.0 2.3 %fusion.8 = f32[512,2,256]{2,0,1:T(8,128)S(1)} fusion(bf16[4096,2,256]{2,1,0:T(2,128)(2,1)S(1)} %bitcast.97, bf16[512,4224]{1,0:T(8,128)(2,1)S(1)} %bitcast.88), kind=kOutput, calls=%fused_computation.12 | convolution fusion | flops 2147483648 | bytes 9437184 | tf_op jit(solution)/shard_map/rd,djf->rjf/dot_general | solution.py:8
  119.4 0.9 fusion.47
  120.2 1.5 collective-permute-start.2
  121.7 0.5 collective-permute-start.1
  122.3 0.0 copy-done.1
  122.3 2.7 %fusion.32 = f32[512,2048]{1,0:T(8,128)} fusion(pred[]{:T(512)S(6)} %eq.61, bf16[1,512,2048]{2,1,0:T(8,128)(2,1)S(1)} %copy-done.1, f32[512,2,256]{2,0,1:T(8,128)S(1)} %fusion.8), kind=kOutput, calls=%fused_computation.46 | convolution fusion | flops 538181632 | bytes 7340033 | tf_op jit(solution)/shard_map/dot_general | solution.py:62
  124.9 0.0 copy-done.2
  124.9 4.3 %fusion.13 = f32[512,2048]{1,0:T(8,128)} fusion(bf16[512,512]{1,0:T(8,128)(2,1)} %fusion.30, pred[]{:T(512)S(6)} %eq.61, bf16[1,1024,2048]{2,1,0:T(8,128)(2,1)S(1)} %copy-done.2), kind=kOutput, calls=%fused_computation.20 | convolution fusion | flops 1074790400 | bytes 8912897 | tf_op jit(solution)/shard_map/dot_general | solution.py:62
  129.2 1.1 slice_convert_fusion
  130.3 0.5 fusion.64
  130.8 0.4 reshape.74
  131.2 0.4 reshape.68
  131.5 0.2 copy.53
  131.7 0.5 select_reduce_fusion.1
  132.3 0.0 collective-permute-done.2
  132.3 3.0 %subtract_convert_fusion = (bf16[512,2048]{1,0:T(8,128)(2,1)S(1)}, bf16[512,2048]{1,0:T(8,128)(2,1)S(1)}) fusion(f32[512,2048]{1,0:T(8,128)} %fusion.32, bf16[512,256]{1,0:T(8,128)(2,1)} %collective-permute-done.2, pred[]{:T(512)S(6)} %eq.61, bf16[1,512,2048]{2,1,0:T(8,128)(2,1)S(1)} %copy-done.1), kind=kOutput, calls=%fused_computation.15 | convolution fusion | flops 542638080 | bytes 10747905 | tf_op jit(solution)/shard_map/dot_general | solution.py:62
  135.3 0.0 copy-start
  135.3 0.0 copy-start.3
  135.3 1.6 fusion.4
  136.9 3.2 %collective-permute-done.1 = bf16[512,512]{1,0:T(8,128)(2,1)S(1)} collective-permute-done((bf16[512,512]{1,0:T(8,128)(2,1)}, bf16[512,512]{1,0:T(8,128)(2,1)S(1)}, u32[]{:S(2)}, u32[]{:S(2)}) %collective-permute-start.1) | collective-permute-done | bytes 524320 | tf_op jit(solution)/shard_map/ppermute | solution.py:57
  140.1 0.0 copy-done
  140.1 0.0 copy-done.3
  140.1 1.4 add_convert_fusion
  141.6 1.3 fusion.68
  142.9 3.7 %fusion.1 = bf16[1024,2048]{1,0:T(8,128)(2,1)} fusion(f32[16,64,2048]{2,1,0:T(8,128)S(1)} %fusion.4, f32[16,64,2048]{2,1,0:T(8,128)S(1)} %fusion.68, f32[1024]{0:T(1024)S(1)} %get-tuple-element.10, f32[1024]{0:T(1024)S(1)} %get-tuple-element.9), kind=kLoop, calls=%fused_computation.3 | loop fusion | flops 8388608 | bytes 20979712 | tf_op jit(solution)/shard_map/convert_element_type | solution.py:147
  146.5 0.0 reduce-scatter.2.cloned.1.call-update
  146.5 70.7 %reduce-scatter.2.cloned.1.call-done = bf16[64,2048]{1,0:T(8,128)(2,1)} async-done(((bf16[1024,2048]{1,0:T(8,128)(2,1)}), bf16[64,2048]{1,0:T(8,128)(2,1)}) %reduce-scatter.2.cloned.1.call-update) | async-done | bytes 262160 | tf_op jit(solution)/shard_map/reduce_scatter | solution.py:147
  (2 shorter events, 0.0 us)
Async XLA Ops:
  6.5 89.6 %all-gather.2.cloned.1.call-start = ((), (), s32[]{:S(2)}) async-start(), calls=%async_computation.1 | async-start | bytes 9191424 | tf_op jit(solution)/shard_map/all_gather | solution.py:89
  6.5 9.5 %collective-permute-start = (bf16[64,2048]{1,0:T(8,128)(2,1)}, bf16[64,2048]{1,0:T(8,128)(2,1)S(1)}, u32[]{:S(2)}, u32[]{:S(2)}) collective-permute-start(bf16[64,2048]{1,0:T(8,128)(2,1)} %param.9), channel_id=1, source_target_pairs={{0,1},{1,0},{2,3},{3,2},{4,5},{5,4},{6,7},{7,6},{8,9},{9,8},{10,11... | collective-permute-start | bytes 786440 | tf_op jit(solution)/shard_map/ppermute | solution.py:46
  17.9 199.3 %reduce-scatter.2.cloned.1.call-start = ((), (), s32[]{:S(2)}) async-start(), calls=%async_computation.2 | async-start | bytes 4456448 | tf_op jit(solution)/shard_map/reduce_scatter | solution.py:147
  108.6 8.4 %copy-start.4 = (bf16[1,4096,2,256]{3,2,1,0:T(2,128)(2,1)S(1)}, bf16[1,4096,2,256]{3,2,1,0:T(2,128)(2,1)}, u32[]{:S(2)}) copy-start(bf16[1,4096,2,256]{3,2,1,0:T(2,128)(2,1)} %param.16) | copy-start | bytes 12582916
  117.0 5.2 %copy-start.1 = (bf16[1,512,2048]{2,1,0:T(8,128)(2,1)S(1)}, bf16[1,512,2048]{2,1,0:T(8,128)(2,1)}, u32[]{:S(2)}) copy-start(bf16[1,512,2048]{2,1,0:T(8,128)(2,1)} %param.17) | copy-start | bytes 6291460
  120.2 4.7 %copy-start.2 = (bf16[1,1024,2048]{2,1,0:T(8,128)(2,1)S(1)}, bf16[1,1024,2048]{2,1,0:T(8,128)(2,1)}, u32[]{:S(2)}) copy-start(bf16[1,1024,2048]{2,1,0:T(8,128)(2,1)} %param.15) | copy-start | bytes 12582916
  120.2 12.0 %collective-permute-start.2 = (bf16[512,256]{1,0:T(8,128)(2,1)}, bf16[512,256]{1,0:T(8,128)(2,1)}, u32[]{:S(2)}, u32[]{:S(2)}) collective-permute-start(bf16[512,256]{1,0:T(8,128)(2,1)} %fusion.47), channel_id=1, source_target_pairs={{0,1},{1,0},{2,3},{3,2},{4,5},{5,4},{6,7},{7,6},{8,9},{9,8},{10,11... | collective-permute-start | bytes 786440 | tf_op jit(solution)/shard_map/ppermute | solution.py:57
  121.7 18.4 %collective-permute-start.1 = (bf16[512,512]{1,0:T(8,128)(2,1)}, bf16[512,512]{1,0:T(8,128)(2,1)S(1)}, u32[]{:S(2)}, u32[]{:S(2)}) collective-permute-start(bf16[512,512]{1,0:T(8,128)(2,1)} %fusion.30), channel_id=1, source_target_pairs={{0,1},{1,0},{2,3},{3,2},{4,5},{5,4},{6,7},{7,6},{8,9},{9,8},{10,11... | collective-permute-start | bytes 1572872 | tf_op jit(solution)/shard_map/ppermute | solution.py:57
  135.3 4.8 %copy-start = (f32[512,2048]{1,0:T(8,128)S(1)}, f32[512,2048]{1,0:T(8,128)}, u32[]{:S(2)}) copy-start(f32[512,2048]{1,0:T(8,128)} %fusion.13) | copy-start | bytes 12582916
  135.3 4.8 %copy-start.3 = (bf16[1,1024,2048]{2,1,0:T(8,128)(2,1)S(1)}, bf16[1,1024,2048]{2,1,0:T(8,128)(2,1)}, u32[]{:S(2)}) copy-start(bf16[1,1024,2048]{2,1,0:T(8,128)(2,1)} %param.15) | copy-start | bytes 12582916
Sparse Core Ops, SparseCore 0:
  18.0 78.0 all-gather.1
  146.7 70.5 reduce-scatter.1
where the time goes:
time: 225 us; the launch traced here: 224 us
  waiting for transfers between devices  150 us (67%)
  matrix products  30.8 us (14%)
  other arithmetic  16.6 us (7%)
  between operations  15.1 us (7%)
  local copies, waits for them, and re-layouts  6.24 us (3%)
  starting transfers between devices  5.04 us (2%)
    all_gather x1, waiting for transfers between devices, per_device(): every_row = lax.all_gather(packed, 'ep', axis=0, tiled=True)  71.5 us
    reduce_scatter x1, waiting for transfers between devices, per_device(): lax.psum_scatter(partial.astype(jnp.bfloat16), 'ep', scatter_dimension=0,...  70.7 us
    dot_general x2, matrix products, gate_up(): jnp.einsum('rd,djf->rjf', row_block, weight, preferred_element_type=jnp.f...  9.58 us
    dot_general x2, matrix products, down_dp(): jnp.dot(hidden, own, preferred_element_type=jnp.float32)  6.95 us
    dot_general x1, matrix products, per_device(): jnp.einsum('gpi,gic->gpc', jnp.concatenate([home_pick, spare_pick], axis=...  5.83 us
    ppermute x1, waiting for transfers between devices, gather_dp(): partner = lax.ppermute(block, 'dp', perm=[(0, 1), (1, 0)])  4.95 us
  transfers between devices with their start and end apart: 5, of which 4 were waited for; matrix products, arithmetic and copies ran while one was open for 10% of the time, Pallas kernels for 0%

commit v1 on v0

--- a/solution.py
+++ b/solution.py
@@ -2,6 +2,12 @@
 import jax.numpy as jnp
 from jax import lax
 from jax.sharding import PartitionSpec as P
+
+
+def in_order(pieces, dim):
+    shape = list(pieces.shape[1:])
+    shape[dim] *= pieces.shape[0]
+    return jnp.moveaxis(pieces, 0, dim).reshape(shape)
 
 
 def gate_up(row_block, weight):
@@ -86,7 +92,19 @@
     d_model = tokens.shape[1] * lax.axis_size("dp")
     whole_rows = gather_dp(tokens, 1)
     packed = jnp.concatenate([whole_rows, side_columns(expert_ids, gate_logits)], axis=1)
-    every_row = lax.all_gather(packed, "ep", axis=0, tiled=True)
+    count = lax.axis_size("ep")
+    pairs = [(i, (i + 1) % count) for i in range(count)]
+    back = [(b, a) for a, b in pairs]
+    lower, upper = ([], [])
+    for turn in range(count - 1):
+        if turn % 2 == 0:
+            lower.append(lax.ppermute(lower[-1] if lower else packed, "ep", pairs))
+        else:
+            upper.append(lax.ppermute(upper[-1] if upper else packed, "ep", back))
+    pieces = jnp.stack([*lower[::-1], packed, *upper])
+    shift = lax.axis_index("ep") - len(lower)
+    pieces = pieces[(jnp.arange(count) - shift) % count]
+    every_row = in_order(pieces, 0)
     all_tokens = every_row.shape[0]
     ids = every_row[:, d_model : d_model + top_count].astype(jnp.int32)
     parts = every_row[:, d_model + top_count : d_model + 4 * top_count].astype(jnp.float32)

time: 225 us -> 289 us (1.28)
  starting transfers between devices: 5.04 us -> 51 us
  local copies, waits for them, and re-layouts: 6.24 us -> 37 us
  waiting for transfers between devices: 150 us -> 135 us
    all_gather x1 -> x0, waiting for transfers between devices: 71.5 us -> none  [per_device(): every_row = lax.all_gather(packed, 'ep', axis=0, tiled=True)]
    ppermute x0 -> x15, waiting for transfers between devices: none -> 46.7 us  [the longest x8 46.7 us: per_device(): lower.append(lax.ppermute(lower[-1] if lower else packed, 'ep', pairs))]
    ppermute x0 -> x15, starting transfers between devices: none -> 45.8 us  [the longest x8 33.9 us: per_device(): lower.append(lax.ppermute(lower[-1] if lower else packed, 'ep', pairs))]
    unnamed x11 -> x41, local copies, waits for them, and re-layouts: 0.12 us -> 21.8 us
    reduce_scatter x1, waiting for transfers between devices: 70.7 us -> 79.7 us  [per_device(): lax.psum_scatter(partial.astype(jnp.bfloat16), 'ep', scatter_dimension=0,...]
    gather x0 -> x1, local copies, waits for them, and re-layouts: none -> 8.39 us  [per_device(): pieces = pieces[(jnp.arange(count) - shift) % count]]
  transfers between devices with their start and end apart: 5 -> 19, of which waited for: 4 -> 10; matrix products, arithmetic and copies ran while one was open for 10% -> 15% of each run, Pallas kernels for 0% -> 0%
where the time goes in v1:
time: 289 us
  waiting for transfers between devices  135 us (47%)
  starting transfers between devices  51 us (18%)
  local copies, waits for them, and re-layouts  37 us (13%)
  matrix products  32 us (11%)
  other arithmetic  17.9 us (6%)
  between operations  15.1 us (5%)
    reduce_scatter x1, waiting for transfers between devices, per_device(): lax.psum_scatter(partial.astype(jnp.bfloat16), 'ep', scatter_dimension=0,...  79.7 us
    ppermute x8, waiting for transfers between devices, per_device(): lower.append(lax.ppermute(lower[-1] if lower else packed, 'ep', pairs))  46.7 us
    ppermute x8, starting transfers between devices, per_device(): lower.append(lax.ppermute(lower[-1] if lower else packed, 'ep', pairs))  33.9 us
    unnamed x41, local copies, waits for them, and re-layouts  21.8 us
    ppermute x7, starting transfers between devices, per_device(): upper.append(lax.ppermute(upper[-1] if upper else packed, 'ep', back))  11.9 us
    dot_general x2, matrix products, gate_up(): jnp.einsum('rd,djf->rjf', row_block, weight, preferred_element_type=jnp.f...  9.78 us
    gather x1, local copies, waits for them, and re-layouts, per_device(): pieces = pieces[(jnp.arange(count) - shift) % count]  8.39 us
    dot_general x2, matrix products, down_dp(): jnp.dot(hidden, own, preferred_element_type=jnp.float32)  7.08 us
  transfers between devices with their start and end apart: 19, of which 10 were waited for; matrix products, arithmetic and copies ran while one was open for 15% of the time, Pallas kernels for 0%

profile of v1, /device:TPU:0, one launch (start us, length us, event | category | flops | bytes accessed | tf_op | source)
XLA Modules:
  0.0 288.6 jit_solution(13253713603189057616)
XLA Ops:
  6.5 3.0 %collective-permute-start = (bf16[64,2048]{1,0:T(8,128)(2,1)}, bf16[64,2048]{1,0:T(8,128)(2,1)S(1)}, u32[]{:S(2)}, u32[]{:S(2)}) collective-permute-start(bf16[64,2048]{1,0:T(8,128)(2,1)} %param.9), channel_id=1, source_target_pairs={{0,1},{1,0},{2,3},{3,2},{4,5},{5,4},{6,7},{7,6},{8,9},{9,8},{10,11... | collective-permute-start | bytes 786440 | tf_op jit(solution)/shard_map/ppermute | solution.py:52
  10.2 0.8 fusion.69
  11.1 4.9 %collective-permute-done = bf16[64,2048]{1,0:T(8,128)(2,1)S(1)} collective-permute-done((bf16[64,2048]{1,0:T(8,128)(2,1)}, bf16[64,2048]{1,0:T(8,128)(2,1)S(1)}, u32[]{:S(2)}, u32[]{:S(2)}) %collective-permute-start) | collective-permute-done | bytes 262176 | tf_op jit(solution)/shard_map/ppermute | solution.py:52
  16.0 1.0 broadcast_select_fusion.1
  17.1 11.5 %collective-permute-done.1 = bf16[64,4224]{1,0:T(8,128)(2,1)S(1)} collective-permute-done((bf16[64,4224]{1,0:T(8,128)(2,1)S(1)}, bf16[64,4224]{1,0:T(8,128)(2,1)S(1)}, u32[]{:S(2)}, u32[]{:S(2)}) %collective-permute-start.1) | collective-permute-done | bytes 540704 | tf_op jit(solution)/shard_map/ppermute | solution.py:101
  28.6 4.4 %collective-permute-start.9 = (bf16[64,4224]{1,0:T(8,128)(2,1)S(1)}, bf16[64,4224]{1,0:T(8,128)(2,1)S(1)}, u32[]{:S(2)}, u32[]{:S(2)}) collective-permute-start(bf16[64,4224]{1,0:T(8,128)(2,1)S(1)} %fusion.42), channel_id=1, source_target_pairs={{2,0},{4,2},{6,4},{8,6},{10,8},{12,10},{14,12},{16,14},{18,16},{20... | collective-permute-start | bytes 1622024 | tf_op jit(solution)/shard_map/ppermute | solution.py:103
  33.0 7.1 %collective-permute-done.2 = bf16[64,4224]{1,0:T(8,128)(2,1)S(1)} collective-permute-done((bf16[64,4224]{1,0:T(8,128)(2,1)S(1)}, bf16[64,4224]{1,0:T(8,128)(2,1)S(1)}, u32[]{:S(2)}, u32[]{:S(2)}) %collective-permute-start.2) | collective-permute-done | bytes 540704 | tf_op jit(solution)/shard_map/ppermute | solution.py:101
  40.2 4.4 %collective-permute-start.10 = (bf16[64,4224]{1,0:T(8,128)(2,1)S(1)}, bf16[64,4224]{1,0:T(8,128)(2,1)S(1)}, u32[]{:S(2)}, u32[]{:S(2)}) collective-permute-start(bf16[64,4224]{1,0:T(8,128)(2,1)S(1)} %collective-permute-done.9), channel_id=1, source_target_pairs={{2,0},{4,2},{6,4},{8,6},{10,8},{12,10},{14,12},{16,14},{18,16},{20... | collective-permute-start | bytes 1622024 | tf_op jit(solution)/shard_map/ppermute | solution.py:103
  44.6 7.1 %collective-permute-done.3 = bf16[64,4224]{1,0:T(8,128)(2,1)S(1)} collective-permute-done((bf16[64,4224]{1,0:T(8,128)(2,1)S(1)}, bf16[64,4224]{1,0:T(8,128)(2,1)S(1)}, u32[]{:S(2)}, u32[]{:S(2)}) %collective-permute-start.3) | collective-permute-done | bytes 540704 | tf_op jit(solution)/shard_map/ppermute | solution.py:101
  51.8 1.9 collective-permute-start.4
  53.6 2.6 collective-permute-start.11
  56.2 7.1 %collective-permute-done.4 = bf16[64,4224]{1,0:T(8,128)(2,1)S(1)} collective-permute-done((bf16[64,4224]{1,0:T(8,128)(2,1)S(1)}, bf16[64,4224]{1,0:T(8,128)(2,1)S(1)}, u32[]{:S(2)}, u32[]{:S(2)}) %collective-permute-start.4) | collective-permute-done | bytes 540704 | tf_op jit(solution)/shard_map/ppermute | solution.py:101
  63.3 4.1 %collective-permute-start.5 = (bf16[64,4224]{1,0:T(8,128)(2,1)S(1)}, bf16[64,4224]{1,0:T(8,128)(2,1)S(1)}, u32[]{:S(2)}, u32[]{:S(2)}) collective-permute-start(bf16[64,4224]{1,0:T(8,128)(2,1)S(1)} %collective-permute-done.4), channel_id=1, source_target_pairs={{0,2},{2,4},{4,6},{6,8},{8,10},{10,12},{12,14},{14,16},{16,18},{18... | collective-permute-start | bytes 1622024 | tf_op jit(solution)/shard_map/ppermute | solution.py:101
  67.4 0.8 copy-done.4
  68.6 6.3 %collective-permute-done.5 = bf16[64,4224]{1,0:T(8,128)(2,1)S(1)} collective-permute-done((bf16[64,4224]{1,0:T(8,128)(2,1)S(1)}, bf16[64,4224]{1,0:T(8,128)(2,1)S(1)}, u32[]{:S(2)}, u32[]{:S(2)}) %collective-permute-start.5) | collective-permute-done | bytes 540704 | tf_op jit(solution)/shard_map/ppermute | solution.py:101
  74.9 7.1 %collective-permute-start.6 = (bf16[64,4224]{1,0:T(8,128)(2,1)S(1)}, bf16[64,4224]{1,0:T(8,128)(2,1)S(1)}, u32[]{:S(2)}, u32[]{:S(2)}) collective-permute-start(bf16[64,4224]{1,0:T(8,128)(2,1)S(1)} %collective-permute-done.5), channel_id=1, source_target_pairs={{0,2},{2,4},{4,6},{6,8},{8,10},{10,12},{12,14},{14,16},{16,18},{18... | collective-permute-start | bytes 1622024 | tf_op jit(solution)/shard_map/ppermute | solution.py:101
  82.0 0.8 copy-done.6
  82.8 3.6 %collective-permute-done.6 = bf16[64,4224]{1,0:T(8,128)(2,1)S(1)} collective-permute-done((bf16[64,4224]{1,0:T(8,128)(2,1)S(1)}, bf16[64,4224]{1,0:T(8,128)(2,1)S(1)}, u32[]{:S(2)}, u32[]{:S(2)}) %collective-permute-start.6) | collective-permute-done | bytes 540704 | tf_op jit(solution)/shard_map/ppermute | solution.py:101
  86.4 10.2 %collective-permute-start.7 = (bf16[64,4224]{1,0:T(8,128)(2,1)S(1)}, bf16[64,4224]{1,0:T(8,128)(2,1)}, u32[]{:S(2)}, u32[]{:S(2)}) collective-permute-start(bf16[64,4224]{1,0:T(8,128)(2,1)S(1)} %collective-permute-done.6), channel_id=1, source_target_pairs={{0,2},{2,4},{4,6},{6,8},{8,10},{10,12},{12,14},{14,16},{16,18},{18... | collective-permute-start | bytes 1622024 | tf_op jit(solution)/shard_map/ppermute | solution.py:101
  96.6 3.9 %collective-permute-done.7 = bf16[64,4224]{1,0:T(8,128)(2,1)} collective-permute-done((bf16[64,4224]{1,0:T(8,128)(2,1)S(1)}, bf16[64,4224]{1,0:T(8,128)(2,1)}, u32[]{:S(2)}, u32[]{:S(2)}) %collective-permute-start.7) | collective-permute-done | bytes 540704 | tf_op jit(solution)/shard_map/ppermute | solution.py:101
  100.5 10.7 %collective-permute-start.8 = (bf16[64,4224]{1,0:T(8,128)(2,1)}, bf16[64,4224]{1,0:T(8,128)(2,1)}, u32[]{:S(2)}, u32[]{:S(2)}) collective-permute-start(bf16[64,4224]{1,0:T(8,128)(2,1)} %collective-permute-done.7), channel_id=1, source_target_pairs={{0,2},{2,4},{4,6},{6,8},{8,10},{10,12},{12,14},{14,16},{16,18},{18... | collective-permute-start | bytes 1622024 | tf_op jit(solution)/shard_map/ppermute | solution.py:101
  111.2 1.2 dynamic_slice.6
  112.4 1.3 dynamic_slice.7
  113.7 1.4 fusion.59
  115.8 1.4 compare_reduce_fusion
  118.0 1.9 bitcast_dynamic-update-slice_fusion.15
  119.9 1.9 bitcast_dynamic-update-slice_fusion.14
  121.8 1.9 bitcast_dynamic-update-slice_fusion.13
  123.7 2.0 bitcast_dynamic-update-slice_fusion.12
  125.6 0.8 bitcast_dynamic-update-slice_fusion.11
  126.5 0.8 bitcast_dynamic-update-slice_fusion.10
  127.3 0.8 bitcast_dynamic-update-slice_fusion.9
  128.2 0.8 bitcast_dynamic-update-slice_fusion.8
  129.0 0.9 bitcast_dynamic-update-slice_fusion.7
  129.8 0.9 bitcast_dynamic-update-slice_fusion.6
  130.7 0.8 bitcast_dynamic-update-slice_fusion.5
  131.5 0.8 bitcast_dynamic-update-slice_fusion.4
  132.4 0.9 bitcast_dynamic-update-slice_fusion.3
  133.2 1.9 bitcast_dynamic-update-slice_fusion.2
  135.1 1.9 bitcast_dynamic-update-slice_fusion.1
  137.0 0.9 bitcast_dynamic-update-slice_fusion
  137.9 8.4 %gather_fusion = bf16[16,64,4224]{2,1,0:T(8,128)(2,1)} fusion(bf16[16,64,4224]{2,1,0:T(8,128)(2,1)} %bitcast_dynamic-update-slice_fusion, s32[1024]{0:T(1024)S(1)} %pad_clamp_fusion), kind=kCustom, calls=%fused_computation | custom fusion | bytes 17301568 | tf_op jit(solution)/shard_map/gather | solution.py:106
  146.3 1.1 slice_convert_fusion
  147.4 1.8 convert_compare_fusion.1
  150.8 0.9 compare_and_fusion
  153.3 5.8 %convolution_convert_fusion = bf16[16,64,4224]{2,1,0:T(8,128)(2,1)S(1)} fusion(bf16[16,64,4224]{2,1,0:T(8,128)(2,1)} %gather_fusion, pred[16,32,64]{2,1,0:T(8,128)(4,1)S(1)} %bitcast.128, pred[16,32,64]{2,1,0:T(8,128)(4,1)S(1)} %bitcast.127), kind=kOutput, calls=%fused_computation.1 | convolution fusion | flops 558039040 | bytes 17367040 | tf_op jit(solution)/shard_map/gpi,gic->gpc/dot_general | solution.py:138
  159.8 7.4 %fusion.2 = f32[512,2,512]{2,0,1:T(8,128)S(1)} fusion(bf16[4096,2,512]{2,1,0:T(2,128)(2,1)} %bitcast.131, bf16[512,4224]{1,0:T(8,128)(2,1)S(1)} %bitcast.124), kind=kOutput, calls=%fused_computation.6 | convolution fusion | flops 4294967296 | bytes 14680064 | tf_op jit(solution)/shard_map/rd,djf->rjf/dot_general | solution.py:14
  167.2 1.1 fusion.30
  168.4 1.5 collective-permute-start.16
  169.9 4.3 %fusion.13 = f32[512,2048]{1,0:T(8,128)} fusion(bf16[512,512]{1,0:T(8,128)(2,1)} %fusion.30, pred[]{:T(512)S(6)} %eq.63, bf16[1,1024,2048]{2,1,0:T(8,128)(2,1)S(1)} %copy-done.2), kind=kOutput, calls=%fused_computation.21 | convolution fusion | flops 1074790400 | bytes 8912897 | tf_op jit(solution)/shard_map/dot_general | solution.py:68
  174.2 2.3 fusion.8
  176.6 0.9 fusion.47
  177.4 2.7 fusion.32
  180.2 0.7 collective-permute-start.17
  180.9 1.1 fusion.66
  182.9 1.2 select_reduce_fusion.1
  184.1 4.1 %collective-permute-done.17 = bf16[512,256]{1,0:T(8,128)(2,1)S(1)} collective-permute-done((bf16[512,256]{1,0:T(8,128)(2,1)}, bf16[512,256]{1,0:T(8,128)(2,1)S(1)}, u32[]{:S(2)}, u32[]{:S(2)}) %collective-permute-start.17) | collective-permute-done | bytes 262176 | tf_op jit(solution)/shard_map/ppermute | solution.py:63
  188.2 2.9 %subtract_convert_fusion = (bf16[512,2048]{1,0:T(8,128)(2,1)S(1)}, bf16[512,2048]{1,0:T(8,128)(2,1)S(1)}) fusion(f32[512,2048]{1,0:T(8,128)} %fusion.32, bf16[512,256]{1,0:T(8,128)(2,1)S(1)} %collective-permute-done.17, pred[]{:T(512)S(6)} %eq.63, bf16[1,512,2048]{2,1,0:T(8,128)(2,1)S(1)} %copy-done.1), kind=kOutput, calls=%fused_computation.16 | convolution fusion | flops 542638080 | bytes 10747905 | tf_op jit(solution)/shard_map/dot_general | solution.py:68
  191.1 1.6 fusion.4
  193.3 1.3 copy-done.3
  194.6 2.4 add_convert_fusion
  197.0 1.3 fusion.70
  198.3 3.7 %fusion.1 = bf16[1024,2048]{1,0:T(8,128)(2,1)} fusion(f32[16,64,2048]{2,1,0:T(8,128)S(1)} %fusion.4, f32[16,64,2048]{2,1,0:T(8,128)S(1)} %fusion.70, f32[1024]{0:T(1024)S(1)} %get-tuple-element.10, f32[1024]{0:T(1024)S(1)} %get-tuple-element.9), kind=kLoop, calls=%fused_computation.4 | loop fusion | flops 8388608 | bytes 20979712 | tf_op jit(solution)/shard_map/convert_element_type | solution.py:165
  202.0 79.7 %reduce-scatter.2.cloned.1.call-done = bf16[64,2048]{1,0:T(8,128)(2,1)} async-done(((bf16[1024,2048]{1,0:T(8,128)(2,1)}), bf16[64,2048]{1,0:T(8,128)(2,1)}) %reduce-scatter.2.cloned.1.call-update) | async-done | bytes 262160 | tf_op jit(solution)/shard_map/reduce_scatter | solution.py:165
  (64 shorter events, 6.7 us)
Async XLA Ops:
  6.5 275.2 %reduce-scatter.2.cloned.1.call-start = ((), (), s32[]{:S(2)}) async-start(), calls=%async_computation.1 | async-start | bytes 4456448 | tf_op jit(solution)/shard_map/reduce_scatter | solution.py:165
  6.5 9.5 %collective-permute-start = (bf16[64,2048]{1,0:T(8,128)(2,1)}, bf16[64,2048]{1,0:T(8,128)(2,1)S(1)}, u32[]{:S(2)}, u32[]{:S(2)}) collective-permute-start(bf16[64,2048]{1,0:T(8,128)(2,1)} %param.9), channel_id=1, source_target_pairs={{0,1},{1,0},{2,3},{3,2},{4,5},{5,4},{6,7},{7,6},{8,9},{9,8},{10,11... | collective-permute-start | bytes 786440 | tf_op jit(solution)/shard_map/ppermute | solution.py:52
  17.1 11.5 %collective-permute-start.1 = (bf16[64,4224]{1,0:T(8,128)(2,1)S(1)}, bf16[64,4224]{1,0:T(8,128)(2,1)S(1)}, u32[]{:S(2)}, u32[]{:S(2)}) collective-permute-start(bf16[64,4224]{1,0:T(8,128)(2,1)S(1)} %fusion.42), channel_id=1, source_target_pairs={{0,2},{2,4},{4,6},{6,8},{8,10},{10,12},{12,14},{14,16},{16,18},{18... | collective-permute-start | bytes 1622024 | tf_op jit(solution)/shard_map/ppermute | solution.py:101
  28.6 11.6 %collective-permute-start.2 = (bf16[64,4224]{1,0:T(8,128)(2,1)S(1)}, bf16[64,4224]{1,0:T(8,128)(2,1)S(1)}, u32[]{:S(2)}, u32[]{:S(2)}) collective-permute-start(bf16[64,4224]{1,0:T(8,128)(2,1)S(1)} %collective-permute-done.1), channel_id=1, source_target_pairs={{0,2},{2,4},{4,6},{6,8},{8,10},{10,12},{12,14},{14,16},{16,18},{18... | collective-permute-start | bytes 1622024 | tf_op jit(solution)/shard_map/ppermute | solution.py:101
  28.6 11.6 %collective-permute-start.9 = (bf16[64,4224]{1,0:T(8,128)(2,1)S(1)}, bf16[64,4224]{1,0:T(8,128)(2,1)S(1)}, u32[]{:S(2)}, u32[]{:S(2)}) collective-permute-start(bf16[64,4224]{1,0:T(8,128)(2,1)S(1)} %fusion.42), channel_id=1, source_target_pairs={{2,0},{4,2},{6,4},{8,6},{10,8},{12,10},{14,12},{16,14},{18,16},{20... | collective-permute-start | bytes 1622024 | tf_op jit(solution)/shard_map/ppermute | solution.py:103
  40.2 11.6 %collective-permute-start.3 = (bf16[64,4224]{1,0:T(8,128)(2,1)S(1)}, bf16[64,4224]{1,0:T(8,128)(2,1)S(1)}, u32[]{:S(2)}, u32[]{:S(2)}) collective-permute-start(bf16[64,4224]{1,0:T(8,128)(2,1)S(1)} %collective-permute-done.2), channel_id=1, source_target_pairs={{0,2},{2,4},{4,6},{6,8},{8,10},{10,12},{12,14},{14,16},{16,18},{18... | collective-permute-start | bytes 1622024 | tf_op jit(solution)/shard_map/ppermute | solution.py:101
  40.2 13.4 %collective-permute-start.10 = (bf16[64,4224]{1,0:T(8,128)(2,1)S(1)}, bf16[64,4224]{1,0:T(8,128)(2,1)S(1)}, u32[]{:S(2)}, u32[]{:S(2)}) collective-permute-start(bf16[64,4224]{1,0:T(8,128)(2,1)S(1)} %collective-permute-done.9), channel_id=1, source_target_pairs={{2,0},{4,2},{6,4},{8,6},{10,8},{12,10},{14,12},{16,14},{18,16},{20... | collective-permute-start | bytes 1622024 | tf_op jit(solution)/shard_map/ppermute | solution.py:103
  51.8 11.6 %collective-permute-start.4 = (bf16[64,4224]{1,0:T(8,128)(2,1)S(1)}, bf16[64,4224]{1,0:T(8,128)(2,1)S(1)}, u32[]{:S(2)}, u32[]{:S(2)}) collective-permute-start(bf16[64,4224]{1,0:T(8,128)(2,1)S(1)} %collective-permute-done.3), channel_id=1, source_target_pairs={{0,2},{2,4},{4,6},{6,8},{8,10},{10,12},{12,14},{14,16},{16,18},{18... | collective-permute-start | bytes 1622024 | tf_op jit(solution)/shard_map/ppermute | solution.py:101
  53.6 13.8 %collective-permute-start.11 = (bf16[64,4224]{1,0:T(8,128)(2,1)S(1)}, bf16[64,4224]{1,0:T(8,128)(2,1)S(1)}, u32[]{:S(2)}, u32[]{:S(2)}) collective-permute-start(bf16[64,4224]{1,0:T(8,128)(2,1)S(1)} %collective-permute-done.10), channel_id=1, source_target_pairs={{2,0},{4,2},{6,4},{8,6},{10,8},{12,10},{14,12},{16,14},{18,16},{20... | collective-permute-start | bytes 1622024 | tf_op jit(solution)/shard_map/ppermute | solution.py:103
  63.3 33.3 %copy-start.8 = (bf16[64,4224]{1,0:T(8,128)(2,1)}, bf16[64,4224]{1,0:T(8,128)(2,1)S(1)}, u32[]{:S(2)}) copy-start(bf16[64,4224]{1,0:T(8,128)(2,1)S(1)} %collective-permute-done.4) | copy-start | bytes 1622020
  63.3 11.6 %collective-permute-start.5 = (bf16[64,4224]{1,0:T(8,128)(2,1)S(1)}, bf16[64,4224]{1,0:T(8,128)(2,1)S(1)}, u32[]{:S(2)}, u32[]{:S(2)}) collective-permute-start(bf16[64,4224]{1,0:T(8,128)(2,1)S(1)} %collective-permute-done.4), channel_id=1, source_target_pairs={{0,2},{2,4},{4,6},{6,8},{8,10},{10,12},{12,14},{14,16},{16,18},{18... | collective-permute-start | bytes 1622024 | tf_op jit(solution)/shard_map/ppermute | solution.py:101
  67.4 0.8 copy-start.4
  68.3 13.7 %collective-permute-start.12 = (bf16[64,4224]{1,0:T(8,128)(2,1)S(1)}, bf16[64,4224]{1,0:T(8,128)(2,1)S(1)}, u32[]{:S(2)}, u32[]{:S(2)}) collective-permute-start(bf16[64,4224]{1,0:T(8,128)(2,1)S(1)} %collective-permute-done.11), channel_id=1, source_target_pairs={{2,0},{4,2},{6,4},{8,6},{10,8},{12,10},{14,12},{16,14},{18,16},{20... | collective-permute-start | bytes 1622024 | tf_op jit(solution)/shard_map/ppermute | solution.py:103
  74.9 21.7 %copy-start.10 = (bf16[64,4224]{1,0:T(8,128)(2,1)}, bf16[64,4224]{1,0:T(8,128)(2,1)S(1)}, u32[]{:S(2)}) copy-start(bf16[64,4224]{1,0:T(8,128)(2,1)S(1)} %collective-permute-done.5) | copy-start | bytes 1622020
  74.9 11.5 %collective-permute-start.6 = (bf16[64,4224]{1,0:T(8,128)(2,1)S(1)}, bf16[64,4224]{1,0:T(8,128)(2,1)S(1)}, u32[]{:S(2)}, u32[]{:S(2)}) collective-permute-start(bf16[64,4224]{1,0:T(8,128)(2,1)S(1)} %collective-permute-done.5), channel_id=1, source_target_pairs={{0,2},{2,4},{4,6},{6,8},{8,10},{10,12},{12,14},{14,16},{16,18},{18... | collective-permute-start | bytes 1622024 | tf_op jit(solution)/shard_map/ppermute | solution.py:101
  82.0 0.8 copy-start.6
  82.8 13.8 %collective-permute-start.13 = (bf16[64,4224]{1,0:T(8,128)(2,1)S(1)}, bf16[64,4224]{1,0:T(8,128)(2,1)}, u32[]{:S(2)}, u32[]{:S(2)}) collective-permute-start(bf16[64,4224]{1,0:T(8,128)(2,1)S(1)} %collective-permute-done.12), channel_id=1, source_target_pairs={{2,0},{4,2},{6,4},{8,6},{10,8},{12,10},{14,12},{16,14},{18,16},{20... | collective-permute-start | bytes 1622024 | tf_op jit(solution)/shard_map/ppermute | solution.py:103
  86.4 14.1 %copy-start.11 = (bf16[64,4224]{1,0:T(8,128)(2,1)}, bf16[64,4224]{1,0:T(8,128)(2,1)S(1)}, u32[]{:S(2)}) copy-start(bf16[64,4224]{1,0:T(8,128)(2,1)S(1)} %collective-permute-done.6) | copy-start | bytes 1622020
  86.4 14.1 %collective-permute-start.7 = (bf16[64,4224]{1,0:T(8,128)(2,1)S(1)}, bf16[64,4224]{1,0:T(8,128)(2,1)}, u32[]{:S(2)}, u32[]{:S(2)}) collective-permute-start(bf16[64,4224]{1,0:T(8,128)(2,1)S(1)} %collective-permute-done.6), channel_id=1, source_target_pairs={{0,2},{2,4},{4,6},{6,8},{8,10},{10,12},{12,14},{14,16},{16,18},{18... | collective-permute-start | bytes 1622024 | tf_op jit(solution)/shard_map/ppermute | solution.py:101
  96.6 21.3 %collective-permute-start.14 = (bf16[64,4224]{1,0:T(8,128)(2,1)}, bf16[64,4224]{1,0:T(8,128)(2,1)}, u32[]{:S(2)}, u32[]{:S(2)}) collective-permute-start(bf16[64,4224]{1,0:T(8,128)(2,1)} %collective-permute-done.13), channel_id=1, source_target_pairs={{2,0},{4,2},{6,4},{8,6},{10,8},{12,10},{14,12},{16,14},{18,16},{20... | collective-permute-start | bytes 1622024 | tf_op jit(solution)/shard_map/ppermute | solution.py:103
  100.5 17.5 %collective-permute-start.8 = (bf16[64,4224]{1,0:T(8,128)(2,1)}, bf16[64,4224]{1,0:T(8,128)(2,1)}, u32[]{:S(2)}, u32[]{:S(2)}) collective-permute-start(bf16[64,4224]{1,0:T(8,128)(2,1)} %collective-permute-done.7), channel_id=1, source_target_pairs={{0,2},{2,4},{4,6},{6,8},{8,10},{10,12},{12,14},{14,16},{16,18},{18... | collective-permute-start | bytes 1622024 | tf_op jit(solution)/shard_map/ppermute | solution.py:101
  117.9 7.8 %copy-start.9 = (bf16[64,4224]{1,0:T(8,128)(2,1)S(1)}, bf16[64,4224]{1,0:T(8,128)(2,1)}, u32[]{:S(2)}) copy-start(bf16[64,4224]{1,0:T(8,128)(2,1)} %copy-done.8) | copy-start | bytes 1622020
  117.9 19.1 %collective-permute-start.15 = (bf16[64,4224]{1,0:T(8,128)(2,1)}, bf16[64,4224]{1,0:T(8,128)(2,1)S(1)}, u32[]{:S(2)}, u32[]{:S(2)}) collective-permute-start(bf16[64,4224]{1,0:T(8,128)(2,1)} %collective-permute-done.14), channel_id=1, source_target_pairs={{2,0},{4,2},{6,4},{8,6},{10,8},{12,10},{14,12},{16,14},{18,16},{20... | collective-permute-start | bytes 1622024 | tf_op jit(solution)/shard_map/ppermute | solution.py:103
  123.7 7.9 %copy-start.5 = (bf16[64,4224]{1,0:T(8,128)(2,1)S(1)}, bf16[64,4224]{1,0:T(8,128)(2,1)}, u32[]{:S(2)}) copy-start(bf16[64,4224]{1,0:T(8,128)(2,1)} %copy-done.4) | copy-start | bytes 1622020
  125.6 6.7 %copy-start.7 = (bf16[64,4224]{1,0:T(8,128)(2,1)S(1)}, bf16[64,4224]{1,0:T(8,128)(2,1)}, u32[]{:S(2)}) copy-start(bf16[64,4224]{1,0:T(8,128)(2,1)} %copy-done.6) | copy-start | bytes 1622020
  159.8 10.1 %copy-start.2 = (bf16[1,1024,2048]{2,1,0:T(8,128)(2,1)S(1)}, bf16[1,1024,2048]{2,1,0:T(8,128)(2,1)}, u32[]{:S(2)}) copy-start(bf16[1,1024,2048]{2,1,0:T(8,128)(2,1)} %param.15) | copy-start | bytes 12582916
  168.4 5.9 %copy-start.12 = (bf16[1,4096,2,256]{3,2,1,0:T(2,128)(2,1)S(1)}, bf16[1,4096,2,256]{3,2,1,0:T(2,128)(2,1)}, u32[]{:S(2)}) copy-start(bf16[1,4096,2,256]{3,2,1,0:T(2,128)(2,1)} %param.16) | copy-start | bytes 12582916
  168.4 24.3 %collective-permute-start.16 = (bf16[512,512]{1,0:T(8,128)(2,1)}, bf16[512,512]{1,0:T(8,128)(2,1)}, u32[]{:S(2)}, u32[]{:S(2)}) collective-permute-start(bf16[512,512]{1,0:T(8,128)(2,1)} %fusion.30), channel_id=1, source_target_pairs={{0,1},{1,0},{2,3},{3,2},{4,5},{5,4},{6,7},{7,6},{8,9},{9,8},{10,11... | collective-permute-start | bytes 1572872 | tf_op jit(solution)/shard_map/ppermute | solution.py:63
  174.2 3.2 %copy-start.1 = (bf16[1,512,2048]{2,1,0:T(8,128)(2,1)S(1)}, bf16[1,512,2048]{2,1,0:T(8,128)(2,1)}, u32[]{:S(2)}) copy-start(bf16[1,512,2048]{2,1,0:T(8,128)(2,1)} %param.17) | copy-start | bytes 6291460
  180.2 8.0 %collective-permute-start.17 = (bf16[512,256]{1,0:T(8,128)(2,1)}, bf16[512,256]{1,0:T(8,128)(2,1)S(1)}, u32[]{:S(2)}, u32[]{:S(2)}) collective-permute-start(bf16[512,256]{1,0:T(8,128)(2,1)} %fusion.47), channel_id=1, source_target_pairs={{0,1},{1,0},{2,3},{3,2},{4,5},{5,4},{6,7},{7,6},{8,9},{9,8},{10,11... | collective-permute-start | bytes 786440 | tf_op jit(solution)/shard_map/ppermute | solution.py:63
  191.1 2.2 copy-start
  191.1 3.5 %copy-start.3 = (bf16[1,1024,2048]{2,1,0:T(8,128)(2,1)S(1)}, bf16[1,1024,2048]{2,1,0:T(8,128)(2,1)}, u32[]{:S(2)}) copy-start(bf16[1,1024,2048]{2,1,0:T(8,128)(2,1)} %param.15) | copy-start | bytes 12582916
Sparse Core Ops, SparseCore 0:
  202.1 79.5 reduce-scatter.1
